TPU v7x, 32 devices: a whole 2x2x4 slice. The times are simulated.
32 devices in a mesh: gx: 8 (over z, x), gy: 4 (over y, core).
Axes of the slice: x: 2, y: 2, z: 4, core: 2. Of those that a mesh axis runs over, the one named last changes fastest.
Arguments:
- patches: bfloat16 [128, 64, 256], P('gx', 'gy'), may hold values from -9 to 9
- w_query: bfloat16 [256, 256], replicated, may hold values from -2 to 2
- w_key: bfloat16 [256, 256], replicated, may hold values from -2 to 2
- w_value: bfloat16 [256, 256], replicated, may hold values from -0.375 to 0.375
- w_out: bfloat16 [256, 256], replicated, may hold values from -0.375 to 0.375
- region_memory: bfloat16 [8, 4, 4, 64, 512], P('gx', 'gy'), may hold values from -6 to 6
- region_owner: int32 [8, 4, 4, 2], P('gx', 'gy'), may hold values from 0 to 7, all different within a row; in each aligned block of 4 rows (0 to 3, 4 to 7, ..., all dimensions but the last counted through in order) at most 2 rows name the same one
- region_local: int32 [8, 4, 4, 2], P('gx', 'gy'), may hold values from 0 to 3
- grad_out: bfloat16 [128, 64, 256], P('gx', 'gy'), may hold values from -6 to 6
Outputs:
- layer_out: bfloat16 [128, 64, 256], P('gx', 'gy')
- grad_patches: bfloat16 [128, 64, 256], P('gx', 'gy')
- grad_w_query: float32 [256, 256], replicated
- grad_w_key: float32 [256, 256], replicated
- grad_w_value: float32 [256, 256], replicated
- grad_w_out: float32 [256, 256], replicated
Inputs may be any that keep to these rules, and one draw needn't show every extreme that they name: `region_owner`: each block names two different owner tiles. The blocks of one tile name one owner at most 2 times, a bound that some tile reaches.
All inputs are finite; a program needn't handle non-finite values.
Results may differ from a plain program's by a relative error of at most 0.02.
Values may be sent and summed in bfloat16 or wider, within the bound.
No kernel may reach another device: no remote copies, remote signals or barrier semaphores. Data moves between devices by JAX's collectives and lax.ppermute only.
A program may use at most 64 MiB of HBM per device.

v0:
```python
import math
import jax
import jax.numpy as jnp
from jax import lax
from jax.sharding import PartitionSpec as P

D = 256
HEADS = 2
HEAD_DIM = 128
BSIDE = 8
BT = 64
masked_score = -1000000000.0


def padded(block, sides, width):
    for axis, dim in sides:
        count = lax.axis_size(axis)
        forward = [(i, i + 1) for i in range(count - 1)]
        backward = [(target, source) for source, target in forward]
        low = lax.ppermute(
            lax.slice_in_dim(block, block.shape[dim] - width, None, axis=dim), axis, forward
        )
        high = lax.ppermute(lax.slice_in_dim(block, 0, width, axis=dim), axis, backward)
        block = jnp.concatenate([low, block, high], axis=dim)
    return block


def to_blocks(grid_array):
    grid_rows, grid_cols, feature_width = grid_array.shape
    shaped = grid_array.reshape(grid_rows // BSIDE, BSIDE, grid_cols // BSIDE, BSIDE, feature_width)
    return shaped.transpose(0, 2, 1, 3, 4).reshape(
        grid_rows // BSIDE, grid_cols // BSIDE, BSIDE * BSIDE, feature_width
    )


def from_blocks(block_array):
    block_rows, block_cols, block_tokens, feature_width = block_array.shape
    shaped = block_array.reshape(block_rows, block_cols, BSIDE, BSIDE, feature_width)
    return shaped.transpose(0, 2, 1, 3, 4).reshape(
        block_rows * BSIDE, block_cols * BSIDE, feature_width
    )


def split_heads(source):
    return source.reshape(source.shape[:-1] + (HEADS, source.shape[-1] // HEADS))


def key_pieces(keyval_pad, key_valid, region_keyval):
    block_rows, block_cols = (region_keyval.shape[0], region_keyval.shape[1])
    pieces = []
    for row_off in range(3):
        for col_off in range(3):
            key_block = keyval_pad[row_off : row_off + block_rows, col_off : col_off + block_cols]
            valid_mask = key_valid[row_off : row_off + block_rows, col_off : col_off + block_cols]
            pieces.append((key_block[..., :D], key_block[..., D:], valid_mask))
    merged = region_keyval.reshape(block_rows, block_cols, 2 * BT, 2 * D)
    pieces.append(
        (merged[..., :D], merged[..., D:], jnp.ones((block_rows, block_cols), dtype=jnp.bool_))
    )
    return pieces


def piece_scores(query_heads, key_part, valid_mask):
    scores = jnp.einsum(
        "abqhe,abkhe->abhqk", query_heads, split_heads(key_part), preferred_element_type=jnp.float32
    )
    scores = scores * (1.0 / math.sqrt(HEAD_DIM))
    return jnp.where(valid_mask[:, :, None, None, None], scores, masked_score)


def attend_forward(query_blocks, keyval_pad, key_valid, region_keyval):
    query_heads = split_heads(query_blocks)
    pieces = key_pieces(keyval_pad, key_valid, region_keyval)
    scores = [
        piece_scores(query_heads, key_part, valid_mask)
        for key_part, value_part, valid_mask in pieces
    ]
    row_top = jnp.max(jnp.concatenate(scores, -1), -1, keepdims=True)
    row_total = sum(
        (jnp.sum(jnp.exp(part_scores - row_top), -1, keepdims=True) for part_scores in scores)
    )
    log_total = row_top + jnp.log(row_total)
    mixed_sum = jnp.zeros(query_heads.shape, jnp.float32)
    for part_scores, (key_part, value_part, valid_mask) in zip(scores, pieces):
        weights = jnp.exp(part_scores - log_total).astype(jnp.bfloat16)
        mixed_sum = mixed_sum + jnp.einsum(
            "abhqk,abkhe->abqhe",
            weights,
            split_heads(value_part),
            preferred_element_type=jnp.float32,
        )
    output = mixed_sum.reshape(query_blocks.shape).astype(jnp.bfloat16)
    return (output, log_total[..., 0])


def query_grads(
    query_blocks, keyval_pad, key_valid, region_keyval, log_total, dout_blocks, delta_rows
):
    query_heads = split_heads(query_blocks)
    dout_heads = split_heads(dout_blocks)
    accum_sum = jnp.zeros(query_heads.shape, jnp.float32)
    for key_part, value_part, valid_mask in key_pieces(keyval_pad, key_valid, region_keyval):
        part_scores = piece_scores(query_heads, key_part, valid_mask)
        prob_part = jnp.exp(part_scores - log_total[..., None])
        grad_prob = jnp.einsum(
            "abqhe,abkhe->abhqk",
            dout_heads,
            split_heads(value_part),
            preferred_element_type=jnp.float32,
        )
        grad_score = (prob_part * (grad_prob - delta_rows[..., None])).astype(jnp.bfloat16)
        accum_sum = accum_sum + jnp.einsum(
            "abhqk,abkhe->abqhe",
            grad_score,
            split_heads(key_part),
            preferred_element_type=jnp.float32,
        )
    return (
        (accum_sum * (1.0 / math.sqrt(HEAD_DIM))).reshape(query_blocks.shape).astype(jnp.bfloat16)
    )


def key_grads(keyval_center, query_pad, dout_pad, log_pad, delta_pad, query_valid):
    block_rows, block_cols = (keyval_center.shape[0], keyval_center.shape[1])
    key_heads = split_heads(keyval_center[..., :D])
    value_heads = split_heads(keyval_center[..., D:])
    grad_key = jnp.zeros(key_heads.shape, jnp.float32)
    grad_value = jnp.zeros(key_heads.shape, jnp.float32)
    for row_off in range(3):
        for col_off in range(3):
            query_heads = split_heads(
                query_pad[row_off : row_off + block_rows, col_off : col_off + block_cols]
            )
            dout_heads = split_heads(
                dout_pad[row_off : row_off + block_rows, col_off : col_off + block_cols]
            )
            log_part = log_pad[row_off : row_off + block_rows, col_off : col_off + block_cols]
            delta_part = delta_pad[row_off : row_off + block_rows, col_off : col_off + block_cols]
            valid_mask = query_valid[row_off : row_off + block_rows, col_off : col_off + block_cols]
            part_scores = jnp.einsum(
                "abqhe,abkhe->abhqk", query_heads, key_heads, preferred_element_type=jnp.float32
            )
            part_scores = part_scores * (1.0 / math.sqrt(HEAD_DIM))
            prob_part = jnp.where(
                valid_mask[:, :, None, None, None], jnp.exp(part_scores - log_part[..., None]), 0.0
            )
            grad_prob = jnp.einsum(
                "abqhe,abkhe->abhqk", dout_heads, value_heads, preferred_element_type=jnp.float32
            )
            grad_score = (prob_part * (grad_prob - delta_part[..., None])).astype(jnp.bfloat16)
            grad_key = grad_key + jnp.einsum(
                "abhqk,abqhe->abkhe", grad_score, query_heads, preferred_element_type=jnp.float32
            )
            rounded_prob = prob_part.astype(jnp.bfloat16)
            grad_value = grad_value + jnp.einsum(
                "abhqk,abqhe->abkhe", rounded_prob, dout_heads, preferred_element_type=jnp.float32
            )
    out_shape = (block_rows, block_cols, BT, D)
    grad_key = (grad_key * (1.0 / math.sqrt(HEAD_DIM))).reshape(out_shape).astype(jnp.bfloat16)
    return (grad_key, grad_value.reshape(out_shape).astype(jnp.bfloat16))


def inner_rows(left_rows, right_rows):
    return lax.dot_general(
        left_rows, right_rows, (((0,), (0,)), ((), ())), preferred_element_type=jnp.float32
    )


def on_device(
    patches, w_query, w_key, w_value, w_out, region_memory, region_owner, region_local, grad_out
):
    tile_rows, tile_cols, model_width = patches.shape
    block_rows, block_cols = (tile_rows // BSIDE, tile_cols // BSIDE)
    block_count = block_rows * block_cols
    flat_in = patches.reshape(-1, model_width)
    w_pair = jnp.concatenate([w_key, w_value], 1)
    queries = jnp.dot(flat_in, w_query, preferred_element_type=jnp.float32).astype(jnp.bfloat16)
    keyvals = jnp.dot(flat_in, w_pair, preferred_element_type=jnp.float32).astype(jnp.bfloat16)
    keyvals = keyvals.reshape(tile_rows, tile_cols, 2 * model_width)
    keyval_grid = padded(keyvals, (("gx", 0), ("gy", 1)), BSIDE)
    keyval_pad = to_blocks(keyval_grid)
    gx_count = lax.axis_size("gx")
    gy_count = lax.axis_size("gy")
    row_ids = lax.axis_index("gx") * block_rows - 1 + jnp.arange(block_rows + 2, dtype=jnp.int32)
    col_ids = lax.axis_index("gy") * block_cols - 1 + jnp.arange(block_cols + 2, dtype=jnp.int32)
    row_valid = (row_ids >= 0) & (row_ids < block_rows * gx_count)
    col_valid = (col_ids >= 0) & (col_ids < block_cols * gy_count)
    key_valid = row_valid[:, None] & col_valid[None, :]
    owners = region_owner.reshape(2 * block_count)
    local_ids = region_local.reshape(2 * block_count)
    memory_local = region_memory.reshape(
        region_memory.shape[2], region_memory.shape[3], region_memory.shape[4]
    )
    region_count = memory_local.shape[0]
    row_tables = lax.all_gather(memory_local, "gx", axis=0, tiled=True)
    fetched = jnp.take(row_tables, owners * region_count + local_ids, axis=0)
    region_keyval = fetched.reshape(
        block_rows, block_cols, 2, memory_local.shape[1], memory_local.shape[2]
    )
    query_blocks = to_blocks(queries.reshape(tile_rows, tile_cols, model_width))
    outputs, log_totals = attend_forward(query_blocks, keyval_pad, key_valid, region_keyval)
    attended = from_blocks(outputs).reshape(-1, model_width)
    layer_out = jnp.dot(attended, w_out, preferred_element_type=jnp.float32).astype(jnp.bfloat16)
    grad_flat = grad_out.reshape(-1, model_width)
    d_attended = jnp.dot(grad_flat, w_out.T, preferred_element_type=jnp.float32).astype(
        jnp.bfloat16
    )
    grad_out_local = inner_rows(attended, grad_flat)
    dout_blocks = to_blocks(d_attended.reshape(tile_rows, tile_cols, model_width))
    delta_rows = jnp.sum(
        split_heads(dout_blocks).astype(jnp.float32) * split_heads(outputs).astype(jnp.float32), -1
    )
    delta_rows = delta_rows.transpose(0, 1, 3, 2)
    d_queries = query_grads(
        query_blocks, keyval_pad, key_valid, region_keyval, log_totals, dout_blocks, delta_rows
    )
    query_grid = jnp.concatenate(
        [
            queries.reshape(tile_rows, tile_cols, model_width),
            d_attended.reshape(tile_rows, tile_cols, model_width),
        ],
        -1,
    )
    query_halo = padded(query_grid, (("gx", 0), ("gy", 1)), BSIDE)
    stat_grid = from_blocks(jnp.concatenate([log_totals, delta_rows], 2).transpose(0, 1, 3, 2))
    stat_halo = padded(stat_grid, (("gx", 0), ("gy", 1)), BSIDE)
    query_all = to_blocks(query_halo)
    stat_pad = to_blocks(stat_halo).transpose(0, 1, 3, 2)
    d_keys, d_values = key_grads(
        keyval_pad[1:-1, 1:-1],
        query_all[..., :model_width],
        query_all[..., model_width:],
        stat_pad[:, :, :HEADS],
        stat_pad[:, :, HEADS:],
        key_valid,
    )
    dq_flat = from_blocks(d_queries).reshape(-1, model_width)
    dk_flat = from_blocks(d_keys).reshape(-1, model_width)
    dv_flat = from_blocks(d_values).reshape(-1, model_width)
    grads_joined = jnp.concatenate([dq_flat, dk_flat, dv_flat], 1)
    w_stacked = jnp.concatenate([w_query.T, w_key.T, w_value.T], 0)
    grad_patches = jnp.dot(grads_joined, w_stacked, preferred_element_type=jnp.float32).astype(
        jnp.bfloat16
    )
    summed = lax.psum(
        (
            inner_rows(flat_in, dq_flat),
            inner_rows(flat_in, dk_flat),
            inner_rows(flat_in, dv_flat),
            grad_out_local,
        ),
        ("gx", "gy"),
    )
    return (
        layer_out.reshape(tile_rows, tile_cols, model_width),
        grad_patches.reshape(tile_rows, tile_cols, model_width),
        summed[0],
        summed[1],
        summed[2],
        summed[3],
    )


def solution(mesh):
    return jax.shard_map(
        on_device,
        mesh=mesh,
        in_specs=(
            P("gx", "gy", None),
            P(),
            P(),
            P(),
            P(),
            P("gx", "gy", None, None, None),
            P("gx", "gy", None, None),
            P("gx", "gy", None, None),
            P("gx", "gy", None),
        ),
        out_specs=(P("gx", "gy", None), P("gx", "gy", None), P(), P(), P(), P()),
        check_vma=False,
    )
```

profile of v0, /device:TPU:0, one launch (start us, length us, event | category | flops | bytes accessed | tf_op | source)
XLA Modules:
  0.0 271.7 jit_solution(11771590287470757042)
XLA Ops:
  7.2 0.7 all-gather.3.cloned.1.call-update
  8.1 1.2 convolution_convert_fusion
  9.3 1.3 collective-permute-start.1
  10.6 5.5 %collective-permute-start = (bf16[8,16,512]{2,1,0:T(8,128)(2,1)S(1)}, bf16[8,16,512]{2,1,0:T(8,128)(2,1)S(1)}, u32[]{:S(2)}, u32[]{:S(2)}) collective-permute-start(bf16[8,16,512]{2,1,0:T(8,128)(2,1)S(1)} %bitcast.503), channel_id=1, source_target_pairs={{0,4},{4,8},{8,12},{12,16},{16,20},{20,24},{24,28},{1,5},{5,9},{9,... | collective-permute-start | bytes 393224 | tf_op jit(solution)/shard_map/ppermute | solution.py:20
  16.1 1.1 convolution_convert_fusion.4
  17.2 1.2 convolution_convert_fusion.2
  18.4 4.8 %collective-permute-start.4 = (bf16[8,16,512]{2,1,0:T(8,128)(2,1)S(1)}, bf16[8,16,512]{2,1,0:T(8,128)(2,1)S(1)}, u32[]{:S(2)}, u32[]{:S(2)}) collective-permute-start(bf16[8,16,512]{2,1,0:T(8,128)(2,1)S(1)} %get-tuple-element.85), channel_id=1, source_target_pairs={{0,4},{4,8},{8,12},{12,16},{16,20},{20,24},{24,28},{1,5},{5,9},{9,... | collective-permute-start | bytes 393224 | tf_op jit(solution)/shard_map/ppermute | solution.py:20
  23.2 1.3 collective-permute-start.5
  25.1 3.5 %collective-permute-done.4 = bf16[8,16,512]{2,1,0:T(8,128)(2,1)S(1)} collective-permute-done((bf16[8,16,512]{2,1,0:T(8,128)(2,1)S(1)}, bf16[8,16,512]{2,1,0:T(8,128)(2,1)S(1)}, u32[]{:S(2)}, u32[]{:S(2)}) %collective-permute-start.4) | collective-permute-done | bytes 131104 | tf_op jit(solution)/shard_map/ppermute | solution.py:20
  28.6 1.5 collective-permute-done.5
  30.2 1.3 collective-permute-start.6
  31.5 1.3 collective-permute-start.7
  33.0 4.8 %collective-permute-start.2 = (bf16[32,8,512]{2,1,0:T(8,128)(2,1)S(1)}, bf16[32,8,512]{2,1,0:T(8,128)(2,1)S(1)}, u32[]{:S(2)}, u32[]{:S(2)}) collective-permute-start(bf16[32,8,512]{2,1,0:T(8,128)(2,1)S(1)} %get-tuple-element.83), channel_id=1, source_target_pairs={{0,1},{1,2},{2,3},{4,5},{5,6},{6,7},{8,9},{9,10},{10,11},{12,13},{... | collective-permute-start | bytes 786440 | tf_op jit(solution)/shard_map/ppermute | solution.py:20
  37.7 1.3 collective-permute-start.3
  39.7 2.8 %collective-permute-done.3 = bf16[32,8,512]{2,1,0:T(8,128)(2,1)} collective-permute-done((bf16[32,8,512]{2,1,0:T(8,128)(2,1)S(1)}, bf16[32,8,512]{2,1,0:T(8,128)(2,1)}, u32[]{:S(2)}, u32[]{:S(2)}) %collective-permute-start.3) | collective-permute-done | bytes 262176 | tf_op jit(solution)/shard_map/ppermute | solution.py:23
  42.5 1.1 pad_maximum_fusion
  43.7 1.2 slice_bitcast_fusion.18
  46.0 0.8 fusion.451
  46.8 0.8 fusion.452
  47.6 0.8 fusion.454
  48.5 0.8 fusion.453
  49.4 0.8 fusion.450
  50.2 1.5 slice_bitcast_fusion
  51.7 13.7 %all-gather.3.cloned.1.call-done = bf16[1,1,32,64,512]{4,3,1,0,2:T(8,128)(2,1)} async-done(((bf16[1,1,4,64,512]{4,3,1,0,2:T(8,128)(2,1)}), bf16[1,1,32,64,512]{4,3,1,0,2:T(8,128)(2,1)}) %all-gather.3.cloned.1.call-update) | async-done | bytes 2097168 | tf_op jit(solution)/shard_map/all_gather | solution.py:195
  65.4 2.2 gather_fusion
  68.1 1.2 fusion.445
  69.3 0.7 maximum_maximum_fusion
  70.4 0.5 exponential_reduce_fusion.8
  70.9 1.2 fusion.118
  74.2 1.0 multiply_reduce_fusion
  75.2 2.1 fusion.84
  77.3 2.2 convolution_add_fusion.24
  79.5 2.2 convolution_add_fusion.23
  81.7 1.4 convolution_add_fusion.22
  83.2 1.3 convolution_add_fusion.21
  84.5 1.3 convolution_add_fusion.20
  85.9 1.3 convolution_add_fusion.19
  88.7 2.4 collective-permute-start.8
  91.5 0.9 fusion.455
  93.0 1.3 collective-permute-start.9
  94.3 4.7 %collective-permute-done.9 = f32[8,16,4]{1,0,2:T(8,128)S(1)} collective-permute-done((f32[8,16,4]{1,0,2:T(8,128)S(1)}, f32[8,16,4]{1,0,2:T(8,128)S(1)}, u32[]{:S(2)}, u32[]{:S(2)}) %collective-permute-start.9) | collective-permute-done | bytes 2080 | tf_op jit(solution)/shard_map/ppermute | solution.py:23
  99.0 1.3 collective-permute-start.10
  100.3 1.5 collective-permute-start.11
  101.8 0.9 convolution_bitcast_fusion.2
  102.8 2.4 collective-permute-done.11
  105.7 0.6 fusion.443
  109.3 0.5 copy-done.24
  111.1 0.8 copy.529
  111.9 1.6 convert_element_type.219
  113.5 1.6 copy.530
  115.1 2.0 convolution_add_fusion.15
  117.1 1.3 convolution_add_fusion.14
  118.5 1.3 convolution_add_fusion.13
  119.7 1.3 convolution_add_fusion.12
  121.0 1.2 convolution_add_fusion.11
  123.6 0.9 convolution_bitcast_fusion.1
  124.5 0.9 convolution_bitcast_fusion
  125.5 0.8 convolution_convert_fusion.3
  126.3 1.0 convolution_convert_fusion.1
  127.3 130.5 %all-reduce.3.cloned.1.call-done = (f32[256,256]{0,1:T(8,128)}, f32[256,256]{0,1:T(8,128)}, f32[256,256]{0,1:T(8,128)}, f32[256,256]{1,0:T(8,128)}) async-done(((f32[256,256]{0,1:T(8,128)}, f32[256,256]{0,1:T(8,128)}, f32[256,256]{0,1:T(8,128)}, f32[256,256]{1,0:T(8,128)}), (f32[256,256]{0,1:T(8,128)}, f32[256,256]{0,1:T(8,128)}, f32[256,256]{0,1:T(8,128)}, ...) | async-done | bytes 1048592 | tf_op jit(solution)/shard_map/psum | solution.py:245
  257.8 1.8 copy.531
  259.6 1.8 copy.532
  261.4 1.8 copy.533
  263.2 1.7 copy.1109
  (262 shorter events, 13.1 us)
Async XLA Ops:
  7.2 17.4 %copy-start.59 = (s32[1,1,4,2]{2,3,1,0:T(2,128)S(1)}, s32[1,1,4,2]{2,3,1,0:T(2,128)}, u32[]{:S(2)}) copy-start(s32[1,1,4,2]{2,3,1,0:T(2,128)} %param.16) | copy-start | bytes 100
  7.2 17.4 %copy-start.60 = (s32[1,1,4,2]{2,3,1,0:T(2,128)S(1)}, s32[1,1,4,2]{2,3,1,0:T(2,128)}, u32[]{:S(2)}) copy-start(s32[1,1,4,2]{2,3,1,0:T(2,128)} %param.15) | copy-start | bytes 100
  7.2 58.2 %all-gather.3.cloned.1.call-start = ((), (), s32[]{:S(2)}) async-start(), calls=%async_computation | async-start | bytes 2359296 | tf_op jit(solution)/shard_map/all_gather | solution.py:195
  7.9 249.9 %all-reduce.3.cloned.1.call-start = ((), (), s32[]{:S(2)}) async-start(), calls=%async_computation.1 | async-start | bytes 2097152 | tf_op jit(solution)/shard_map/psum | solution.py:245
  9.3 23.5 %collective-permute-start.1 = (bf16[8,16,512]{2,1,0:T(8,128)(2,1)S(1)}, bf16[8,16,512]{2,1,0:T(8,128)(2,1)S(1)}, u32[]{:S(2)}, u32[]{:S(2)}) collective-permute-start(bf16[8,16,512]{2,1,0:T(8,128)(2,1)S(1)} %bitcast.504), channel_id=1, source_target_pairs={{4,0},{8,4},{12,8},{16,12},{20,16},{24,20},{28,24},{5,1},{9,5},{13... | collective-permute-start | bytes 393224 | tf_op jit(solution)/shard_map/ppermute | solution.py:23
  10.6 22.2 %collective-permute-start = (bf16[8,16,512]{2,1,0:T(8,128)(2,1)S(1)}, bf16[8,16,512]{2,1,0:T(8,128)(2,1)S(1)}, u32[]{:S(2)}, u32[]{:S(2)}) collective-permute-start(bf16[8,16,512]{2,1,0:T(8,128)(2,1)S(1)} %bitcast.503), channel_id=1, source_target_pairs={{0,4},{4,8},{8,12},{12,16},{16,20},{20,24},{24,28},{1,5},{5,9},{9,... | collective-permute-start | bytes 393224 | tf_op jit(solution)/shard_map/ppermute | solution.py:20
  18.4 10.2 %collective-permute-start.4 = (bf16[8,16,512]{2,1,0:T(8,128)(2,1)S(1)}, bf16[8,16,512]{2,1,0:T(8,128)(2,1)S(1)}, u32[]{:S(2)}, u32[]{:S(2)}) collective-permute-start(bf16[8,16,512]{2,1,0:T(8,128)(2,1)S(1)} %get-tuple-element.85), channel_id=1, source_target_pairs={{0,4},{4,8},{8,12},{12,16},{16,20},{20,24},{24,28},{1,5},{5,9},{9,... | collective-permute-start | bytes 393224 | tf_op jit(solution)/shard_map/ppermute | solution.py:20
  23.2 6.9 %collective-permute-start.5 = (bf16[8,16,512]{2,1,0:T(8,128)(2,1)S(1)}, bf16[8,16,512]{2,1,0:T(8,128)(2,1)S(1)}, u32[]{:S(2)}, u32[]{:S(2)}) collective-permute-start(bf16[8,16,512]{2,1,0:T(8,128)(2,1)S(1)} %get-tuple-element.86), channel_id=1, source_target_pairs={{4,0},{8,4},{12,8},{16,12},{20,16},{24,20},{28,24},{5,1},{9,5},{13... | collective-permute-start | bytes 393224 | tf_op jit(solution)/shard_map/ppermute | solution.py:23
  25.0 20.0 %copy-start.75 = (pred[2,2]{1,0:T(4,128)(4,1)}, pred[2,2]{1,0:T(4,128)(4,1)S(1)}, u32[]{:S(2)}) copy-start(pred[2,2]{1,0:T(4,128)(4,1)S(1)} %get-tuple-element.112) | copy-start | bytes 16
  25.0 20.3 %copy-start.73 = (pred[2,2]{1,0:T(4,128)(4,1)}, pred[2,2]{1,0:T(4,128)(4,1)S(1)}, u32[]{:S(2)}) copy-start(pred[2,2]{1,0:T(4,128)(4,1)S(1)} %get-tuple-element.113) | copy-start | bytes 16
  25.0 20.5 %copy-start.71 = (pred[2,2]{1,0:T(4,128)(4,1)}, pred[2,2]{1,0:T(4,128)(4,1)S(1)}, u32[]{:S(2)}) copy-start(pred[2,2]{1,0:T(4,128)(4,1)S(1)} %get-tuple-element.114) | copy-start | bytes 16
  25.0 20.7 %copy-start.69 = (pred[2,2]{1,0:T(4,128)(4,1)}, pred[2,2]{1,0:T(4,128)(4,1)S(1)}, u32[]{:S(2)}) copy-start(pred[2,2]{1,0:T(4,128)(4,1)S(1)} %get-tuple-element.115) | copy-start | bytes 16
  25.0 20.9 %copy-start.65 = (pred[2,2]{1,0:T(4,128)(4,1)}, pred[2,2]{1,0:T(4,128)(4,1)S(1)}, u32[]{:S(2)}) copy-start(pred[2,2]{1,0:T(4,128)(4,1)S(1)} %get-tuple-element.117) | copy-start | bytes 16
  25.0 21.8 %copy-start.63 = (pred[2,2]{1,0:T(4,128)(4,1)}, pred[2,2]{1,0:T(4,128)(4,1)S(1)}, u32[]{:S(2)}) copy-start(pred[2,2]{1,0:T(4,128)(4,1)S(1)} %get-tuple-element.118) | copy-start | bytes 16
  25.1 22.6 %copy-start.61 = (pred[2,2]{1,0:T(4,128)(4,1)}, pred[2,2]{1,0:T(4,128)(4,1)S(1)}, u32[]{:S(2)}) copy-start(pred[2,2]{1,0:T(4,128)(4,1)S(1)} %get-tuple-element.111) | copy-start | bytes 16
  25.1 23.4 %copy-start.77 = (pred[2,2]{1,0:T(4,128)(4,1)}, pred[2,2]{1,0:T(4,128)(4,1)S(1)}, u32[]{:S(2)}) copy-start(pred[2,2]{1,0:T(4,128)(4,1)S(1)} %get-tuple-element.119) | copy-start | bytes 16
  25.1 24.3 %copy-start.67 = (pred[2,2]{1,0:T(4,128)(4,1)}, pred[2,2]{1,0:T(4,128)(4,1)S(1)}, u32[]{:S(2)}) copy-start(pred[2,2]{1,0:T(4,128)(4,1)S(1)} %get-tuple-element.116) | copy-start | bytes 16
  30.2 9.3 %collective-permute-start.6 = (bf16[32,8,512]{2,1,0:T(8,128)(2,1)S(1)}, bf16[32,8,512]{2,1,0:T(8,128)(2,1)S(1)}, u32[]{:S(2)}, u32[]{:S(2)}) collective-permute-start(bf16[32,8,512]{2,1,0:T(8,128)(2,1)S(1)} %get-tuple-element.79), channel_id=1, source_target_pairs={{0,1},{1,2},{2,3},{4,5},{5,6},{6,7},{8,9},{9,10},{10,11},{12,13},{... | collective-permute-start | bytes 786440 | tf_op jit(solution)/shard_map/ppermute | solution.py:20
  31.5 8.0 %collective-permute-start.7 = (bf16[32,8,512]{2,1,0:T(8,128)(2,1)S(1)}, bf16[32,8,512]{2,1,0:T(8,128)(2,1)S(1)}, u32[]{:S(2)}, u32[]{:S(2)}) collective-permute-start(bf16[32,8,512]{2,1,0:T(8,128)(2,1)S(1)} %get-tuple-element.80), channel_id=1, source_target_pairs={{1,0},{2,1},{3,2},{5,4},{6,5},{7,6},{9,8},{10,9},{11,10},{13,12},{... | collective-permute-start | bytes 786440 | tf_op jit(solution)/shard_map/ppermute | solution.py:23
  33.0 6.8 %collective-permute-start.2 = (bf16[32,8,512]{2,1,0:T(8,128)(2,1)S(1)}, bf16[32,8,512]{2,1,0:T(8,128)(2,1)S(1)}, u32[]{:S(2)}, u32[]{:S(2)}) collective-permute-start(bf16[32,8,512]{2,1,0:T(8,128)(2,1)S(1)} %get-tuple-element.83), channel_id=1, source_target_pairs={{0,1},{1,2},{2,3},{4,5},{5,6},{6,7},{8,9},{9,10},{10,11},{12,13},{... | collective-permute-start | bytes 786440 | tf_op jit(solution)/shard_map/ppermute | solution.py:20
  37.7 4.8 %collective-permute-start.3 = (bf16[32,8,512]{2,1,0:T(8,128)(2,1)S(1)}, bf16[32,8,512]{2,1,0:T(8,128)(2,1)}, u32[]{:S(2)}, u32[]{:S(2)}) collective-permute-start(bf16[32,8,512]{2,1,0:T(8,128)(2,1)S(1)} %get-tuple-element.84), channel_id=1, source_target_pairs={{1,0},{2,1},{3,2},{5,4},{6,5},{7,6},{9,8},{10,9},{11,10},{13,12},{... | collective-permute-start | bytes 786440 | tf_op jit(solution)/shard_map/ppermute | solution.py:23
  39.4 9.9 %copy-start.48 = (bf16[2,2,64,2,128]{4,3,2,1,0:T(2,128)(2,1)}, bf16[2,2,64,2,128]{4,3,2,1,0:T(2,128)(2,1)S(1)}, u32[]{:S(2)}) copy-start(bf16[2,2,64,2,128]{4,3,2,1,0:T(2,128)(2,1)S(1)} %reshape_reshape.29) | copy-start | bytes 393220
  44.9 4.3 %copy-start.38 = (bf16[2,2,8,2,8,128]{5,4,3,2,1,0:T(8,128)(2,1)}, bf16[2,2,8,2,8,128]{5,4,3,2,1,0:T(8,128)(2,1)S(1)}, u32[]{:S(2)}) copy-start(bf16[2,2,8,2,8,128]{5,4,3,2,1,0:T(8,128)(2,1)S(1)} %get-tuple-element.69) | copy-start | bytes 393220
  45.0 4.3 %copy-start.40 = (bf16[2,2,8,2,8,128]{5,4,3,2,1,0:T(8,128)(2,1)}, bf16[2,2,8,2,8,128]{5,4,3,2,1,0:T(8,128)(2,1)S(1)}, u32[]{:S(2)}) copy-start(bf16[2,2,8,2,8,128]{5,4,3,2,1,0:T(8,128)(2,1)S(1)} %get-tuple-element.70) | copy-start | bytes 393220
  45.0 4.3 %copy-start.42 = (bf16[2,2,8,2,8,128]{5,4,3,2,1,0:T(8,128)(2,1)}, bf16[2,2,8,2,8,128]{5,4,3,2,1,0:T(8,128)(2,1)S(1)}, u32[]{:S(2)}) copy-start(bf16[2,2,8,2,8,128]{5,4,3,2,1,0:T(8,128)(2,1)S(1)} %get-tuple-element.71) | copy-start | bytes 393220
  45.0 4.3 %copy-start.43 = (bf16[2,2,8,2,8,128]{5,4,3,2,1,0:T(8,128)(2,1)}, bf16[2,2,8,2,8,128]{5,4,3,2,1,0:T(8,128)(2,1)S(1)}, u32[]{:S(2)}) copy-start(bf16[2,2,8,2,8,128]{5,4,3,2,1,0:T(8,128)(2,1)S(1)} %get-tuple-element.72) | copy-start | bytes 393220
  45.0 4.3 %copy-start.44 = (bf16[2,2,8,2,8,128]{5,4,3,2,1,0:T(8,128)(2,1)}, bf16[2,2,8,2,8,128]{5,4,3,2,1,0:T(8,128)(2,1)S(1)}, u32[]{:S(2)}) copy-start(bf16[2,2,8,2,8,128]{5,4,3,2,1,0:T(8,128)(2,1)S(1)} %get-tuple-element.74) | copy-start | bytes 393220
  45.0 4.3 %copy-start.45 = (bf16[2,2,8,2,8,128]{5,4,3,2,1,0:T(8,128)(2,1)}, bf16[2,2,8,2,8,128]{5,4,3,2,1,0:T(8,128)(2,1)S(1)}, u32[]{:S(2)}) copy-start(bf16[2,2,8,2,8,128]{5,4,3,2,1,0:T(8,128)(2,1)S(1)} %get-tuple-element.75) | copy-start | bytes 393220
  45.0 4.3 %copy-start.46 = (bf16[2,2,8,2,8,128]{5,4,3,2,1,0:T(8,128)(2,1)}, bf16[2,2,8,2,8,128]{5,4,3,2,1,0:T(8,128)(2,1)S(1)}, u32[]{:S(2)}) copy-start(bf16[2,2,8,2,8,128]{5,4,3,2,1,0:T(8,128)(2,1)S(1)} %get-tuple-element.76) | copy-start | bytes 393220
  45.0 4.3 %copy-start.47 = (bf16[2,2,8,2,8,128]{5,4,3,2,1,0:T(8,128)(2,1)}, bf16[2,2,8,2,8,128]{5,4,3,2,1,0:T(8,128)(2,1)S(1)}, u32[]{:S(2)}) copy-start(bf16[2,2,8,2,8,128]{5,4,3,2,1,0:T(8,128)(2,1)S(1)} %get-tuple-element.77) | copy-start | bytes 393220
  45.0 4.3 %copy-start.32 = (bf16[2,2,8,2,8,128]{5,4,3,2,1,0:T(8,128)(2,1)}, bf16[2,2,8,2,8,128]{5,4,3,2,1,0:T(8,128)(2,1)S(1)}, u32[]{:S(2)}) copy-start(bf16[2,2,8,2,8,128]{5,4,3,2,1,0:T(8,128)(2,1)S(1)} %get-tuple-element.73) | copy-start | bytes 393220
  68.1 4.0 %copy-start.20 = (bf16[2,2,8,2,8,128]{5,4,3,2,1,0:T(8,128)(2,1)S(1)}, bf16[2,2,8,2,8,128]{5,4,3,2,1,0:T(8,128)(2,1)}, u32[]{:S(2)}) copy-start(bf16[2,2,8,2,8,128]{5,4,3,2,1,0:T(8,128)(2,1)} %get-tuple-element.68) | copy-start | bytes 393220
  70.3 2.3 copy-start.17
  70.9 2.3 copy-start.15
  77.3 4.5 %copy-start.18 = (bf16[2,2,8,2,8,128]{5,4,3,2,1,0:T(8,128)(2,1)S(1)}, bf16[2,2,8,2,8,128]{5,4,3,2,1,0:T(8,128)(2,1)}, u32[]{:S(2)}) copy-start(bf16[2,2,8,2,8,128]{5,4,3,2,1,0:T(8,128)(2,1)} %get-tuple-element.66) | copy-start | bytes 393220
  79.5 5.0 %copy-start.16 = (bf16[2,2,8,2,8,128]{5,4,3,2,1,0:T(8,128)(2,1)S(1)}, bf16[2,2,8,2,8,128]{5,4,3,2,1,0:T(8,128)(2,1)}, u32[]{:S(2)}) copy-start(bf16[2,2,8,2,8,128]{5,4,3,2,1,0:T(8,128)(2,1)} %get-tuple-element.64) | copy-start | bytes 393220
  79.5 6.4 %copy-start.14 = (bf16[2,2,8,2,8,128]{5,4,3,2,1,0:T(8,128)(2,1)S(1)}, bf16[2,2,8,2,8,128]{5,4,3,2,1,0:T(8,128)(2,1)}, u32[]{:S(2)}) copy-start(bf16[2,2,8,2,8,128]{5,4,3,2,1,0:T(8,128)(2,1)} %get-tuple-element.63) | copy-start | bytes 393220
  81.7 5.5 %copy-start.12 = (bf16[2,2,8,2,8,128]{5,4,3,2,1,0:T(8,128)(2,1)S(1)}, bf16[2,2,8,2,8,128]{5,4,3,2,1,0:T(8,128)(2,1)}, u32[]{:S(2)}) copy-start(bf16[2,2,8,2,8,128]{5,4,3,2,1,0:T(8,128)(2,1)} %get-tuple-element.62) | copy-start | bytes 393220
  83.2 4.5 %copy-start.10 = (bf16[2,2,8,2,8,128]{5,4,3,2,1,0:T(8,128)(2,1)S(1)}, bf16[2,2,8,2,8,128]{5,4,3,2,1,0:T(8,128)(2,1)}, u32[]{:S(2)}) copy-start(bf16[2,2,8,2,8,128]{5,4,3,2,1,0:T(8,128)(2,1)} %get-tuple-element.61) | copy-start | bytes 393220
  84.5 2.7 copy-start.41
  84.5 3.1 %copy-start.39 = (bf16[2,2,8,2,8,128]{5,4,3,2,1,0:T(8,128)(2,1)S(1)}, bf16[2,2,8,2,8,128]{5,4,3,2,1,0:T(8,128)(2,1)}, u32[]{:S(2)}) copy-start(bf16[2,2,8,2,8,128]{5,4,3,2,1,0:T(8,128)(2,1)} %copy-done.38) | copy-start | bytes 393220
  87.2 3.9 %copy-start.55 = (bf16[2,2,64,2,128]{4,2,3,1,0:T(8,128)(2,1)S(1)}, bf16[2,2,64,2,128]{4,2,3,1,0:T(8,128)(2,1)}, u32[]{:S(2)}) copy-start(bf16[2,2,64,2,128]{4,2,3,1,0:T(8,128)(2,1)} %get-tuple-element.141) | copy-start | bytes 393220
  87.7 3.8 %copy-start.49 = (bf16[16,16,256]{2,1,0:T(8,128)(2,1)S(1)}, bf16[16,16,256]{2,1,0:T(8,128)(2,1)}, u32[]{:S(2)}) copy-start(bf16[16,16,256]{2,1,0:T(8,128)(2,1)} %param.17) | copy-start | bytes 393220
  88.7 5.5 %collective-permute-start.8 = (f32[8,16,4]{1,0,2:T(8,128)S(1)}, f32[8,16,4]{1,0,2:T(8,128)S(1)}, u32[]{:S(2)}, u32[]{:S(2)}) collective-permute-start(f32[8,16,4]{1,0,2:T(8,128)S(1)} %slice.401), channel_id=1, source_target_pairs={{0,4},{4,8},{8,12},{12,16},{16,20},{20,24},{24,28},{1,5},{5,9},{9,... | collective-permute-start | bytes 6152 | tf_op jit(solution)/shard_map/ppermute | solution.py:20
  91.4 14.9 %copy-start.33 = (bf16[2,2,8,2,8,128]{5,4,3,2,1,0:T(8,128)(2,1)S(1)}, bf16[2,2,8,2,8,128]{5,4,3,2,1,0:T(8,128)(2,1)}, u32[]{:S(2)}) copy-start(bf16[2,2,8,2,8,128]{5,4,3,2,1,0:T(8,128)(2,1)} %copy-done.32) | copy-start | bytes 393220
  91.5 14.9 %copy-start.37 = (bf16[2,2,8,2,8,128]{5,4,3,2,1,0:T(8,128)(2,1)S(1)}, bf16[2,2,8,2,8,128]{5,4,3,2,1,0:T(8,128)(2,1)}, u32[]{:S(2)}) copy-start(bf16[2,2,8,2,8,128]{5,4,3,2,1,0:T(8,128)(2,1)} %get-tuple-element.60) | copy-start | bytes 393220
  91.5 14.9 %copy-start.78 = (pred[2,2]{1,0:T(4,128)(4,1)S(1)}, pred[2,2]{1,0:T(4,128)(4,1)}, u32[]{:S(2)}) copy-start(pred[2,2]{1,0:T(4,128)(4,1)} %copy-done.77) | copy-start | bytes 16
  92.5 14.1 %copy-start.8 = (bf16[2,2,8,2,8,128]{5,4,3,2,1,0:T(8,128)(2,1)S(1)}, bf16[2,2,8,2,8,128]{5,4,3,2,1,0:T(8,128)(2,1)}, u32[]{:S(2)}) copy-start(bf16[2,2,8,2,8,128]{5,4,3,2,1,0:T(8,128)(2,1)} %get-tuple-element.59) | copy-start | bytes 393220
  92.7 13.8 %copy-start.50 = (bf16[2,8,2,8,256]{4,3,2,1,0:T(8,128)(2,1)}, bf16[2,8,2,8,256]{4,3,2,1,0:T(8,128)(2,1)S(1)}, u32[]{:S(2)}) copy-start(bf16[2,8,2,8,256]{4,3,2,1,0:T(8,128)(2,1)S(1)} %copy.449) | copy-start | bytes 393220
  93.0 6.0 %collective-permute-start.9 = (f32[8,16,4]{1,0,2:T(8,128)S(1)}, f32[8,16,4]{1,0,2:T(8,128)S(1)}, u32[]{:S(2)}, u32[]{:S(2)}) collective-permute-start(f32[8,16,4]{1,0,2:T(8,128)S(1)} %slice.403), channel_id=1, source_target_pairs={{4,0},{8,4},{12,8},{16,12},{20,16},{24,20},{28,24},{5,1},{9,5},{13... | collective-permute-start | bytes 6152 | tf_op jit(solution)/shard_map/ppermute | solution.py:23
  99.0 3.7 %collective-permute-start.10 = (f32[32,8,4]{1,0,2:T(8,128)S(1)}, f32[32,8,4]{1,0,2:T(8,128)S(1)}, u32[]{:S(2)}, u32[]{:S(2)}) collective-permute-start(f32[32,8,4]{1,0,2:T(8,128)S(1)} %get-tuple-element.89), channel_id=1, source_target_pairs={{0,1},{1,2},{2,3},{4,5},{5,6},{6,7},{8,9},{9,10},{10,11},{12,13},{... | collective-permute-start | bytes 12296 | tf_op jit(solution)/shard_map/ppermute | solution.py:20
  100.3 4.8 %collective-permute-start.11 = (f32[32,8,4]{1,0,2:T(8,128)S(1)}, f32[32,8,4]{1,0,2:T(8,128)S(1)}, u32[]{:S(2)}, u32[]{:S(2)}) collective-permute-start(f32[32,8,4]{1,0,2:T(8,128)S(1)} %get-tuple-element.90), channel_id=1, source_target_pairs={{1,0},{2,1},{3,2},{5,4},{6,5},{7,6},{9,8},{10,9},{11,10},{13,12},{... | collective-permute-start | bytes 12296 | tf_op jit(solution)/shard_map/ppermute | solution.py:23
  101.8 5.3 %copy-start.53 = (bf16[2,2,8,2,8,128]{5,4,3,2,1,0:T(8,128)(2,1)S(1)}, bf16[2,2,8,2,8,128]{5,4,3,2,1,0:T(8,128)(2,1)}, u32[]{:S(2)}) copy-start(bf16[2,2,8,2,8,128]{5,4,3,2,1,0:T(8,128)(2,1)} %get-tuple-element.44) | copy-start | bytes 393220
  101.8 5.3 %copy-start.76 = (pred[2,2]{1,0:T(4,128)(4,1)S(1)}, pred[2,2]{1,0:T(4,128)(4,1)}, u32[]{:S(2)}) copy-start(pred[2,2]{1,0:T(4,128)(4,1)} %copy-done.75) | copy-start | bytes 16
  110.5 6.6 %copy-start.23 = (f32[2,2,2,64,64]{3,4,2,1,0:T(8,128)S(1)}, f32[2,2,2,64,64]{3,4,2,1,0:T(8,128)}, u32[]{:S(2)}) copy-start(f32[2,2,2,64,64]{3,4,2,1,0:T(8,128)} %copy-done.22) | copy-start | bytes 393220
  118.4 3.8 %copy-start.29 = (bf16[2,2,8,2,8,128]{5,4,3,2,1,0:T(8,128)(2,1)S(1)}, bf16[2,2,8,2,8,128]{5,4,3,2,1,0:T(8,128)(2,1)}, u32[]{:S(2)}) copy-start(bf16[2,2,8,2,8,128]{5,4,3,2,1,0:T(8,128)(2,1)} %get-tuple-element.48) | copy-start | bytes 393220
  118.5 4.1 %copy-start.27 = (bf16[2,2,8,2,8,128]{5,4,3,2,1,0:T(8,128)(2,1)S(1)}, bf16[2,2,8,2,8,128]{5,4,3,2,1,0:T(8,128)(2,1)}, u32[]{:S(2)}) copy-start(bf16[2,2,8,2,8,128]{5,4,3,2,1,0:T(8,128)(2,1)} %get-tuple-element.46) | copy-start | bytes 393220
  119.7 3.2 %copy-start.54 = (bf16[2,2,8,2,8,128]{5,4,3,2,1,0:T(8,128)(2,1)S(1)}, bf16[2,2,8,2,8,128]{5,4,3,2,1,0:T(8,128)(2,1)}, u32[]{:S(2)}) copy-start(bf16[2,2,8,2,8,128]{5,4,3,2,1,0:T(8,128)(2,1)} %get-tuple-element.44) | copy-start | bytes 393220
  122.2 2.3 copy-start.52
  122.9 2.5 copy-start.25
  122.9 3.4 %copy-start.51 = (bf16[2,8,2,8,256]{4,3,2,1,0:T(8,128)(2,1)S(1)}, bf16[2,8,2,8,256]{4,3,2,1,0:T(8,128)(2,1)}, u32[]{:S(2)}) copy-start(bf16[2,8,2,8,256]{4,3,2,1,0:T(8,128)(2,1)} %copy-done.50) | copy-start | bytes 393220
  122.9 3.4 %copy-start.56 = (bf16[256,256]{1,0:T(8,128)(2,1)S(1)}, bf16[256,256]{1,0:T(8,128)(2,1)}, u32[]{:S(2)}) copy-start(bf16[256,256]{1,0:T(8,128)(2,1)} %param.12) | copy-start | bytes 393220
  123.0 3.4 %copy-start.57 = (bf16[256,256]{1,0:T(8,128)(2,1)S(1)}, bf16[256,256]{1,0:T(8,128)(2,1)}, u32[]{:S(2)}) copy-start(bf16[256,256]{1,0:T(8,128)(2,1)} %param.11) | copy-start | bytes 393220
  123.0 3.4 %copy-start.58 = (bf16[256,256]{1,0:T(8,128)(2,1)S(1)}, bf16[256,256]{1,0:T(8,128)(2,1)}, u32[]{:S(2)}) copy-start(bf16[256,256]{1,0:T(8,128)(2,1)} %param.10) | copy-start | bytes 393220
  (29 other events, 44.3 us)
Sparse Core Ops, SparseCore 0:
  10.2 55.1 all-gather.2
  125.6 132.2 all-reduce.2
where the time goes:
time: 273 us; the launch traced here: 272 us
  waiting for transfers between devices  160 us (59%)
  matrix products  44.2 us (16%)
  starting transfers between devices  28.1 us (10%)
  local copies, waits for them, and re-layouts  20.5 us (8%)
  between operations  15.9 us (6%)
  other arithmetic  3.19 us (1%)
    psum x1, waiting for transfers between devices, on_device(): lax.psum((inner_rows(flat_in, dq_flat), inner_rows(flat_in, dk_flat), inn...  131 us
    ppermute x6, starting transfers between devices, padded(): lax.ppermute(lax.slice_in_dim(block, block.shape[dim] - width, None, axis...  20.1 us
    all_gather x1, waiting for transfers between devices, on_device(): row_tables = lax.all_gather(memory_local, 'gx', axis=0, tiled=True)  13.7 us
    dot_general x10, matrix products, query_grads(): jnp.einsum('abhqk,abkhe->abqhe', grad_score, split_heads(key_part), prefe...  13.1 us
    ppermute x6, waiting for transfers between devices, padded(): lax.ppermute(lax.slice_in_dim(block, 0, width, axis=dim), axis, backward)  11.4 us
    unnamed x166, local copies, waits for them, and re-layouts  10.8 us
    dot_general x9, matrix products, key_grads(): jnp.einsum('abhqk,abqhe->abkhe', grad_score, query_heads, preferred_eleme...  8.38 us
    ppermute x6, starting transfers between devices, padded(): lax.ppermute(lax.slice_in_dim(block, 0, width, axis=dim), axis, backward)  7.92 us
  transfers between devices with their start and end apart: 14, of which 7 were waited for; matrix products, arithmetic and copies ran while one was open for 7% of the time, Pallas kernels for 0%

commit v1 on v0

--- a/solution.py
+++ b/solution.py
@@ -243,13 +243,16 @@
         jnp.bfloat16
     )
     summed = lax.psum(
-        (
-            inner_rows(flat_in, dq_flat),
-            inner_rows(flat_in, dk_flat),
-            inner_rows(flat_in, dv_flat),
-            grad_out_local,
+        lax.psum(
+            (
+                inner_rows(flat_in, dq_flat),
+                inner_rows(flat_in, dk_flat),
+                inner_rows(flat_in, dv_flat),
+                grad_out_local,
+            ),
+            "gy",
         ),
-        ("gx", "gy"),
+        "gx",
     )
     return (
         layer_out.reshape(tile_rows, tile_cols, model_width),

time: 273 us -> 262 us (0.960)
  waiting for transfers between devices: 160 us -> 149 us
    psum x1, waiting for transfers between devices: 131 us -> 38.2 us  [on_device(): lax.psum((inner_rows(flat_in, dq_flat), inner_rows(flat_in, dk_flat), inn...]
    psum x0 -> x1, waiting for transfers between devices: none -> 81.9 us  [on_device(): lax.psum(lax.psum((inner_rows(flat_in, dq_flat), inner_rows(flat_in, dk_f...]
  transfers between devices with their start and end apart: 14 -> 15, of which waited for: 7 -> 8; matrix products, arithmetic and copies ran while one was open for 7% -> 7% of each run, Pallas kernels for 0% -> 0%
where the time goes in v1:
time: 262 us; the launch traced here: 261 us
  waiting for transfers between devices  149 us (57%)
  matrix products  44.2 us (17%)
  starting transfers between devices  28.2 us (11%)
  local copies, waits for them, and re-layouts  20.5 us (8%)
  between operations  15.6 us (6%)
  other arithmetic  3.19 us (1%)
    psum x1, waiting for transfers between devices, on_device(): lax.psum(lax.psum((inner_rows(flat_in, dq_flat), inner_rows(flat_in, dk_f...  81.9 us
    psum x1, waiting for transfers between devices, on_device(): lax.psum((inner_rows(flat_in, dq_flat), inner_rows(flat_in, dk_flat), inn...  38.2 us
    ppermute x6, starting transfers between devices, padded(): lax.ppermute(lax.slice_in_dim(block, block.shape[dim] - width, None, axis...  20.1 us
    all_gather x1, waiting for transfers between devices, on_device(): row_tables = lax.all_gather(memory_local, 'gx', axis=0, tiled=True)  13.6 us
    dot_general x10, matrix products, query_grads(): jnp.einsum('abhqk,abkhe->abqhe', grad_score, split_heads(key_part), prefe...  13.1 us
    ppermute x6, waiting for transfers between devices, padded(): lax.ppermute(lax.slice_in_dim(block, 0, width, axis=dim), axis, backward)  11.4 us
    unnamed x166, local copies, waits for them, and re-layouts  10.8 us
    dot_general x9, matrix products, key_grads(): jnp.einsum('abhqk,abqhe->abkhe', grad_score, query_heads, preferred_eleme...  8.38 us
  transfers between devices with their start and end apart: 15, of which 8 were waited for; matrix products, arithmetic and copies ran while one was open for 7% of the time, Pallas kernels for 0%

profile of v1, /device:TPU:0, one launch (start us, length us, event | category | flops | bytes accessed | tf_op | source)
XLA Modules:
  0.0 261.0 jit_solution(17470101024480476024)
XLA Ops:
  7.2 0.7 all-gather.3.cloned.1.call-update
  8.1 1.2 convolution_convert_fusion
  9.3 1.3 collective-permute-start.1
  10.6 5.5 %collective-permute-start = (bf16[8,16,512]{2,1,0:T(8,128)(2,1)S(1)}, bf16[8,16,512]{2,1,0:T(8,128)(2,1)S(1)}, u32[]{:S(2)}, u32[]{:S(2)}) collective-permute-start(bf16[8,16,512]{2,1,0:T(8,128)(2,1)S(1)} %bitcast.503), channel_id=1, source_target_pairs={{0,4},{4,8},{8,12},{12,16},{16,20},{20,24},{24,28},{1,5},{5,9},{9,... | collective-permute-start | bytes 393224 | tf_op jit(solution)/shard_map/ppermute | solution.py:20
  16.1 1.1 convolution_convert_fusion.4
  17.2 1.2 convolution_convert_fusion.2
  18.4 4.8 %collective-permute-start.4 = (bf16[8,16,512]{2,1,0:T(8,128)(2,1)S(1)}, bf16[8,16,512]{2,1,0:T(8,128)(2,1)S(1)}, u32[]{:S(2)}, u32[]{:S(2)}) collective-permute-start(bf16[8,16,512]{2,1,0:T(8,128)(2,1)S(1)} %get-tuple-element.89), channel_id=1, source_target_pairs={{0,4},{4,8},{8,12},{12,16},{16,20},{20,24},{24,28},{1,5},{5,9},{9,... | collective-permute-start | bytes 393224 | tf_op jit(solution)/shard_map/ppermute | solution.py:20
  23.2 1.3 collective-permute-start.5
  25.1 3.5 %collective-permute-done.4 = bf16[8,16,512]{2,1,0:T(8,128)(2,1)S(1)} collective-permute-done((bf16[8,16,512]{2,1,0:T(8,128)(2,1)S(1)}, bf16[8,16,512]{2,1,0:T(8,128)(2,1)S(1)}, u32[]{:S(2)}, u32[]{:S(2)}) %collective-permute-start.4) | collective-permute-done | bytes 131104 | tf_op jit(solution)/shard_map/ppermute | solution.py:20
  28.6 1.5 collective-permute-done.5
  30.2 1.3 collective-permute-start.6
  31.5 1.3 collective-permute-start.7
  33.0 4.8 %collective-permute-start.2 = (bf16[32,8,512]{2,1,0:T(8,128)(2,1)S(1)}, bf16[32,8,512]{2,1,0:T(8,128)(2,1)S(1)}, u32[]{:S(2)}, u32[]{:S(2)}) collective-permute-start(bf16[32,8,512]{2,1,0:T(8,128)(2,1)S(1)} %get-tuple-element.87), channel_id=1, source_target_pairs={{0,1},{1,2},{2,3},{4,5},{5,6},{6,7},{8,9},{9,10},{10,11},{12,13},{... | collective-permute-start | bytes 786440 | tf_op jit(solution)/shard_map/ppermute | solution.py:20
  37.7 1.3 collective-permute-start.3
  39.7 2.8 %collective-permute-done.3 = bf16[32,8,512]{2,1,0:T(8,128)(2,1)} collective-permute-done((bf16[32,8,512]{2,1,0:T(8,128)(2,1)S(1)}, bf16[32,8,512]{2,1,0:T(8,128)(2,1)}, u32[]{:S(2)}, u32[]{:S(2)}) %collective-permute-start.3) | collective-permute-done | bytes 262176 | tf_op jit(solution)/shard_map/ppermute | solution.py:23
  42.5 1.1 pad_maximum_fusion
  43.7 1.2 slice_bitcast_fusion.18
  46.0 0.8 fusion.451
  46.8 0.8 fusion.452
  47.6 0.8 fusion.454
  48.5 0.8 fusion.453
  49.4 0.8 fusion.450
  50.2 1.5 slice_bitcast_fusion
  51.7 13.6 %all-gather.3.cloned.1.call-done = bf16[1,1,32,64,512]{4,3,1,0,2:T(8,128)(2,1)} async-done(((bf16[1,1,4,64,512]{4,3,1,0,2:T(8,128)(2,1)}), bf16[1,1,32,64,512]{4,3,1,0,2:T(8,128)(2,1)}) %all-gather.3.cloned.1.call-update) | async-done | bytes 2097168 | tf_op jit(solution)/shard_map/all_gather | solution.py:195
  65.4 2.2 gather_fusion
  68.1 1.2 fusion.445
  69.3 0.7 maximum_maximum_fusion
  70.3 0.5 exponential_reduce_fusion.8
  70.9 1.2 fusion.118
  74.2 1.0 multiply_reduce_fusion
  75.2 2.1 fusion.84
  77.3 2.2 convolution_add_fusion.24
  79.5 2.2 convolution_add_fusion.23
  81.7 1.4 convolution_add_fusion.22
  83.2 1.3 convolution_add_fusion.21
  84.5 1.3 convolution_add_fusion.20
  85.9 1.3 convolution_add_fusion.19
  88.7 2.4 collective-permute-start.8
  91.5 0.9 fusion.455
  93.0 1.3 collective-permute-start.9
  94.3 4.7 %collective-permute-done.9 = f32[8,16,4]{1,0,2:T(8,128)S(1)} collective-permute-done((f32[8,16,4]{1,0,2:T(8,128)S(1)}, f32[8,16,4]{1,0,2:T(8,128)S(1)}, u32[]{:S(2)}, u32[]{:S(2)}) %collective-permute-start.9) | collective-permute-done | bytes 2080 | tf_op jit(solution)/shard_map/ppermute | solution.py:23
  99.1 1.3 collective-permute-start.10
  100.4 1.5 collective-permute-start.11
  101.9 0.9 convolution_bitcast_fusion.2
  102.8 2.4 collective-permute-done.11
  105.7 0.6 fusion.443
  111.1 0.8 copy.529
  111.9 1.6 convert_element_type.219
  113.5 1.6 copy.530
  115.1 2.0 convolution_add_fusion.15
  117.1 1.3 convolution_add_fusion.14
  118.5 1.3 convolution_add_fusion.13
  119.8 1.3 convolution_add_fusion.12
  121.0 1.2 convolution_add_fusion.11
  123.6 0.9 convolution_bitcast_fusion.1
  124.5 0.9 convolution_bitcast_fusion
  125.5 38.2 %all-reduce.7.cloned.1.call-done = (f32[256,256]{0,1:T(8,128)}, f32[256,256]{0,1:T(8,128)}, f32[256,256]{0,1:T(8,128)}, f32[256,256]{1,0:T(8,128)}) async-done(((f32[256,256]{0,1:T(8,128)}, f32[256,256]{0,1:T(8,128)}, f32[256,256]{0,1:T(8,128)}, f32[256,256]{1,0:T(8,128)}), (f32[256,256]{0,1:T(8,128)}, f32[256,256]{0,1:T(8,128)}, f32[256,256]{0,1:T(8,128)}, ...) | async-done | bytes 1048592 | tf_op jit(solution)/shard_map/psum | solution.py:246
  163.8 0.8 convolution_convert_fusion.3
  164.6 1.0 convolution_convert_fusion.1
  165.6 81.9 %all-reduce.5.cloned.1.call-done = (f32[256,256]{0,1:T(8,128)}, f32[256,256]{0,1:T(8,128)}, f32[256,256]{0,1:T(8,128)}, f32[256,256]{1,0:T(8,128)}) async-done(((f32[256,256]{0,1:T(8,128)}, f32[256,256]{0,1:T(8,128)}, f32[256,256]{0,1:T(8,128)}, f32[256,256]{1,0:T(8,128)}), (f32[256,256]{0,1:T(8,128)}, f32[256,256]{0,1:T(8,128)}, f32[256,256]{0,1:T(8,128)}, ...) | async-done | bytes 1048592 | tf_op jit(solution)/shard_map/psum | solution.py:245
  247.5 1.8 copy.531
  249.3 1.8 copy.532
  251.1 1.8 copy.533
  252.8 1.7 copy.1113
  (265 shorter events, 13.6 us)
Async XLA Ops:
  7.2 17.4 %copy-start.59 = (s32[1,1,4,2]{2,3,1,0:T(2,128)S(1)}, s32[1,1,4,2]{2,3,1,0:T(2,128)}, u32[]{:S(2)}) copy-start(s32[1,1,4,2]{2,3,1,0:T(2,128)} %param.16) | copy-start | bytes 100
  7.2 17.4 %copy-start.60 = (s32[1,1,4,2]{2,3,1,0:T(2,128)S(1)}, s32[1,1,4,2]{2,3,1,0:T(2,128)}, u32[]{:S(2)}) copy-start(s32[1,1,4,2]{2,3,1,0:T(2,128)} %param.15) | copy-start | bytes 100
  7.2 58.2 %all-gather.3.cloned.1.call-start = ((), (), s32[]{:S(2)}) async-start(), calls=%async_computation | async-start | bytes 2359296 | tf_op jit(solution)/shard_map/all_gather | solution.py:195
  7.9 155.8 %all-reduce.7.cloned.1.call-start = ((), (), s32[]{:S(2)}) async-start(), calls=%async_computation.2 | async-start | bytes 2097152 | tf_op jit(solution)/shard_map/psum | solution.py:246
  9.3 23.5 %collective-permute-start.1 = (bf16[8,16,512]{2,1,0:T(8,128)(2,1)S(1)}, bf16[8,16,512]{2,1,0:T(8,128)(2,1)S(1)}, u32[]{:S(2)}, u32[]{:S(2)}) collective-permute-start(bf16[8,16,512]{2,1,0:T(8,128)(2,1)S(1)} %bitcast.504), channel_id=1, source_target_pairs={{4,0},{8,4},{12,8},{16,12},{20,16},{24,20},{28,24},{5,1},{9,5},{13... | collective-permute-start | bytes 393224 | tf_op jit(solution)/shard_map/ppermute | solution.py:23
  10.6 22.2 %collective-permute-start = (bf16[8,16,512]{2,1,0:T(8,128)(2,1)S(1)}, bf16[8,16,512]{2,1,0:T(8,128)(2,1)S(1)}, u32[]{:S(2)}, u32[]{:S(2)}) collective-permute-start(bf16[8,16,512]{2,1,0:T(8,128)(2,1)S(1)} %bitcast.503), channel_id=1, source_target_pairs={{0,4},{4,8},{8,12},{12,16},{16,20},{20,24},{24,28},{1,5},{5,9},{9,... | collective-permute-start | bytes 393224 | tf_op jit(solution)/shard_map/ppermute | solution.py:20
  18.4 10.2 %collective-permute-start.4 = (bf16[8,16,512]{2,1,0:T(8,128)(2,1)S(1)}, bf16[8,16,512]{2,1,0:T(8,128)(2,1)S(1)}, u32[]{:S(2)}, u32[]{:S(2)}) collective-permute-start(bf16[8,16,512]{2,1,0:T(8,128)(2,1)S(1)} %get-tuple-element.89), channel_id=1, source_target_pairs={{0,4},{4,8},{8,12},{12,16},{16,20},{20,24},{24,28},{1,5},{5,9},{9,... | collective-permute-start | bytes 393224 | tf_op jit(solution)/shard_map/ppermute | solution.py:20
  23.2 6.9 %collective-permute-start.5 = (bf16[8,16,512]{2,1,0:T(8,128)(2,1)S(1)}, bf16[8,16,512]{2,1,0:T(8,128)(2,1)S(1)}, u32[]{:S(2)}, u32[]{:S(2)}) collective-permute-start(bf16[8,16,512]{2,1,0:T(8,128)(2,1)S(1)} %get-tuple-element.90), channel_id=1, source_target_pairs={{4,0},{8,4},{12,8},{16,12},{20,16},{24,20},{28,24},{5,1},{9,5},{13... | collective-permute-start | bytes 393224 | tf_op jit(solution)/shard_map/ppermute | solution.py:23
  25.0 20.0 %copy-start.75 = (pred[2,2]{1,0:T(4,128)(4,1)}, pred[2,2]{1,0:T(4,128)(4,1)S(1)}, u32[]{:S(2)}) copy-start(pred[2,2]{1,0:T(4,128)(4,1)S(1)} %get-tuple-element.116) | copy-start | bytes 16
  25.0 20.3 %copy-start.73 = (pred[2,2]{1,0:T(4,128)(4,1)}, pred[2,2]{1,0:T(4,128)(4,1)S(1)}, u32[]{:S(2)}) copy-start(pred[2,2]{1,0:T(4,128)(4,1)S(1)} %get-tuple-element.117) | copy-start | bytes 16
  25.0 20.5 %copy-start.71 = (pred[2,2]{1,0:T(4,128)(4,1)}, pred[2,2]{1,0:T(4,128)(4,1)S(1)}, u32[]{:S(2)}) copy-start(pred[2,2]{1,0:T(4,128)(4,1)S(1)} %get-tuple-element.118) | copy-start | bytes 16
  25.0 20.7 %copy-start.69 = (pred[2,2]{1,0:T(4,128)(4,1)}, pred[2,2]{1,0:T(4,128)(4,1)S(1)}, u32[]{:S(2)}) copy-start(pred[2,2]{1,0:T(4,128)(4,1)S(1)} %get-tuple-element.119) | copy-start | bytes 16
  25.0 20.9 %copy-start.65 = (pred[2,2]{1,0:T(4,128)(4,1)}, pred[2,2]{1,0:T(4,128)(4,1)S(1)}, u32[]{:S(2)}) copy-start(pred[2,2]{1,0:T(4,128)(4,1)S(1)} %get-tuple-element.121) | copy-start | bytes 16
  25.0 21.8 %copy-start.63 = (pred[2,2]{1,0:T(4,128)(4,1)}, pred[2,2]{1,0:T(4,128)(4,1)S(1)}, u32[]{:S(2)}) copy-start(pred[2,2]{1,0:T(4,128)(4,1)S(1)} %get-tuple-element.122) | copy-start | bytes 16
  25.1 22.6 %copy-start.61 = (pred[2,2]{1,0:T(4,128)(4,1)}, pred[2,2]{1,0:T(4,128)(4,1)S(1)}, u32[]{:S(2)}) copy-start(pred[2,2]{1,0:T(4,128)(4,1)S(1)} %get-tuple-element.115) | copy-start | bytes 16
  25.1 23.4 %copy-start.77 = (pred[2,2]{1,0:T(4,128)(4,1)}, pred[2,2]{1,0:T(4,128)(4,1)S(1)}, u32[]{:S(2)}) copy-start(pred[2,2]{1,0:T(4,128)(4,1)S(1)} %get-tuple-element.123) | copy-start | bytes 16
  25.1 24.3 %copy-start.67 = (pred[2,2]{1,0:T(4,128)(4,1)}, pred[2,2]{1,0:T(4,128)(4,1)S(1)}, u32[]{:S(2)}) copy-start(pred[2,2]{1,0:T(4,128)(4,1)S(1)} %get-tuple-element.120) | copy-start | bytes 16
  30.2 9.3 %collective-permute-start.6 = (bf16[32,8,512]{2,1,0:T(8,128)(2,1)S(1)}, bf16[32,8,512]{2,1,0:T(8,128)(2,1)S(1)}, u32[]{:S(2)}, u32[]{:S(2)}) collective-permute-start(bf16[32,8,512]{2,1,0:T(8,128)(2,1)S(1)} %get-tuple-element.83), channel_id=1, source_target_pairs={{0,1},{1,2},{2,3},{4,5},{5,6},{6,7},{8,9},{9,10},{10,11},{12,13},{... | collective-permute-start | bytes 786440 | tf_op jit(solution)/shard_map/ppermute | solution.py:20
  31.5 8.0 %collective-permute-start.7 = (bf16[32,8,512]{2,1,0:T(8,128)(2,1)S(1)}, bf16[32,8,512]{2,1,0:T(8,128)(2,1)S(1)}, u32[]{:S(2)}, u32[]{:S(2)}) collective-permute-start(bf16[32,8,512]{2,1,0:T(8,128)(2,1)S(1)} %get-tuple-element.84), channel_id=1, source_target_pairs={{1,0},{2,1},{3,2},{5,4},{6,5},{7,6},{9,8},{10,9},{11,10},{13,12},{... | collective-permute-start | bytes 786440 | tf_op jit(solution)/shard_map/ppermute | solution.py:23
  33.0 6.8 %collective-permute-start.2 = (bf16[32,8,512]{2,1,0:T(8,128)(2,1)S(1)}, bf16[32,8,512]{2,1,0:T(8,128)(2,1)S(1)}, u32[]{:S(2)}, u32[]{:S(2)}) collective-permute-start(bf16[32,8,512]{2,1,0:T(8,128)(2,1)S(1)} %get-tuple-element.87), channel_id=1, source_target_pairs={{0,1},{1,2},{2,3},{4,5},{5,6},{6,7},{8,9},{9,10},{10,11},{12,13},{... | collective-permute-start | bytes 786440 | tf_op jit(solution)/shard_map/ppermute | solution.py:20
  37.7 4.8 %collective-permute-start.3 = (bf16[32,8,512]{2,1,0:T(8,128)(2,1)S(1)}, bf16[32,8,512]{2,1,0:T(8,128)(2,1)}, u32[]{:S(2)}, u32[]{:S(2)}) collective-permute-start(bf16[32,8,512]{2,1,0:T(8,128)(2,1)S(1)} %get-tuple-element.88), channel_id=1, source_target_pairs={{1,0},{2,1},{3,2},{5,4},{6,5},{7,6},{9,8},{10,9},{11,10},{13,12},{... | collective-permute-start | bytes 786440 | tf_op jit(solution)/shard_map/ppermute | solution.py:23
  39.4 9.9 %copy-start.48 = (bf16[2,2,64,2,128]{4,3,2,1,0:T(2,128)(2,1)}, bf16[2,2,64,2,128]{4,3,2,1,0:T(2,128)(2,1)S(1)}, u32[]{:S(2)}) copy-start(bf16[2,2,64,2,128]{4,3,2,1,0:T(2,128)(2,1)S(1)} %reshape_reshape.29) | copy-start | bytes 393220
  44.9 4.3 %copy-start.38 = (bf16[2,2,8,2,8,128]{5,4,3,2,1,0:T(8,128)(2,1)}, bf16[2,2,8,2,8,128]{5,4,3,2,1,0:T(8,128)(2,1)S(1)}, u32[]{:S(2)}) copy-start(bf16[2,2,8,2,8,128]{5,4,3,2,1,0:T(8,128)(2,1)S(1)} %get-tuple-element.73) | copy-start | bytes 393220
  45.0 4.3 %copy-start.40 = (bf16[2,2,8,2,8,128]{5,4,3,2,1,0:T(8,128)(2,1)}, bf16[2,2,8,2,8,128]{5,4,3,2,1,0:T(8,128)(2,1)S(1)}, u32[]{:S(2)}) copy-start(bf16[2,2,8,2,8,128]{5,4,3,2,1,0:T(8,128)(2,1)S(1)} %get-tuple-element.74) | copy-start | bytes 393220
  45.0 4.3 %copy-start.42 = (bf16[2,2,8,2,8,128]{5,4,3,2,1,0:T(8,128)(2,1)}, bf16[2,2,8,2,8,128]{5,4,3,2,1,0:T(8,128)(2,1)S(1)}, u32[]{:S(2)}) copy-start(bf16[2,2,8,2,8,128]{5,4,3,2,1,0:T(8,128)(2,1)S(1)} %get-tuple-element.75) | copy-start | bytes 393220
  45.0 4.3 %copy-start.43 = (bf16[2,2,8,2,8,128]{5,4,3,2,1,0:T(8,128)(2,1)}, bf16[2,2,8,2,8,128]{5,4,3,2,1,0:T(8,128)(2,1)S(1)}, u32[]{:S(2)}) copy-start(bf16[2,2,8,2,8,128]{5,4,3,2,1,0:T(8,128)(2,1)S(1)} %get-tuple-element.76) | copy-start | bytes 393220
  45.0 4.3 %copy-start.44 = (bf16[2,2,8,2,8,128]{5,4,3,2,1,0:T(8,128)(2,1)}, bf16[2,2,8,2,8,128]{5,4,3,2,1,0:T(8,128)(2,1)S(1)}, u32[]{:S(2)}) copy-start(bf16[2,2,8,2,8,128]{5,4,3,2,1,0:T(8,128)(2,1)S(1)} %get-tuple-element.78) | copy-start | bytes 393220
  45.0 4.3 %copy-start.45 = (bf16[2,2,8,2,8,128]{5,4,3,2,1,0:T(8,128)(2,1)}, bf16[2,2,8,2,8,128]{5,4,3,2,1,0:T(8,128)(2,1)S(1)}, u32[]{:S(2)}) copy-start(bf16[2,2,8,2,8,128]{5,4,3,2,1,0:T(8,128)(2,1)S(1)} %get-tuple-element.79) | copy-start | bytes 393220
  45.0 4.3 %copy-start.46 = (bf16[2,2,8,2,8,128]{5,4,3,2,1,0:T(8,128)(2,1)}, bf16[2,2,8,2,8,128]{5,4,3,2,1,0:T(8,128)(2,1)S(1)}, u32[]{:S(2)}) copy-start(bf16[2,2,8,2,8,128]{5,4,3,2,1,0:T(8,128)(2,1)S(1)} %get-tuple-element.80) | copy-start | bytes 393220
  45.0 4.3 %copy-start.47 = (bf16[2,2,8,2,8,128]{5,4,3,2,1,0:T(8,128)(2,1)}, bf16[2,2,8,2,8,128]{5,4,3,2,1,0:T(8,128)(2,1)S(1)}, u32[]{:S(2)}) copy-start(bf16[2,2,8,2,8,128]{5,4,3,2,1,0:T(8,128)(2,1)S(1)} %get-tuple-element.81) | copy-start | bytes 393220
  45.0 4.3 %copy-start.32 = (bf16[2,2,8,2,8,128]{5,4,3,2,1,0:T(8,128)(2,1)}, bf16[2,2,8,2,8,128]{5,4,3,2,1,0:T(8,128)(2,1)S(1)}, u32[]{:S(2)}) copy-start(bf16[2,2,8,2,8,128]{5,4,3,2,1,0:T(8,128)(2,1)S(1)} %get-tuple-element.77) | copy-start | bytes 393220
  68.1 4.0 %copy-start.20 = (bf16[2,2,8,2,8,128]{5,4,3,2,1,0:T(8,128)(2,1)S(1)}, bf16[2,2,8,2,8,128]{5,4,3,2,1,0:T(8,128)(2,1)}, u32[]{:S(2)}) copy-start(bf16[2,2,8,2,8,128]{5,4,3,2,1,0:T(8,128)(2,1)} %get-tuple-element.72) | copy-start | bytes 393220
  70.3 2.3 copy-start.17
  77.3 4.5 %copy-start.18 = (bf16[2,2,8,2,8,128]{5,4,3,2,1,0:T(8,128)(2,1)S(1)}, bf16[2,2,8,2,8,128]{5,4,3,2,1,0:T(8,128)(2,1)}, u32[]{:S(2)}) copy-start(bf16[2,2,8,2,8,128]{5,4,3,2,1,0:T(8,128)(2,1)} %get-tuple-element.70) | copy-start | bytes 393220
  79.5 5.0 %copy-start.16 = (bf16[2,2,8,2,8,128]{5,4,3,2,1,0:T(8,128)(2,1)S(1)}, bf16[2,2,8,2,8,128]{5,4,3,2,1,0:T(8,128)(2,1)}, u32[]{:S(2)}) copy-start(bf16[2,2,8,2,8,128]{5,4,3,2,1,0:T(8,128)(2,1)} %get-tuple-element.68) | copy-start | bytes 393220
  79.5 6.4 %copy-start.14 = (bf16[2,2,8,2,8,128]{5,4,3,2,1,0:T(8,128)(2,1)S(1)}, bf16[2,2,8,2,8,128]{5,4,3,2,1,0:T(8,128)(2,1)}, u32[]{:S(2)}) copy-start(bf16[2,2,8,2,8,128]{5,4,3,2,1,0:T(8,128)(2,1)} %get-tuple-element.67) | copy-start | bytes 393220
  81.7 5.5 %copy-start.12 = (bf16[2,2,8,2,8,128]{5,4,3,2,1,0:T(8,128)(2,1)S(1)}, bf16[2,2,8,2,8,128]{5,4,3,2,1,0:T(8,128)(2,1)}, u32[]{:S(2)}) copy-start(bf16[2,2,8,2,8,128]{5,4,3,2,1,0:T(8,128)(2,1)} %get-tuple-element.66) | copy-start | bytes 393220
  83.2 4.5 %copy-start.10 = (bf16[2,2,8,2,8,128]{5,4,3,2,1,0:T(8,128)(2,1)S(1)}, bf16[2,2,8,2,8,128]{5,4,3,2,1,0:T(8,128)(2,1)}, u32[]{:S(2)}) copy-start(bf16[2,2,8,2,8,128]{5,4,3,2,1,0:T(8,128)(2,1)} %get-tuple-element.65) | copy-start | bytes 393220
  84.5 2.7 %copy-start.41 = (bf16[2,2,8,2,8,128]{5,4,3,2,1,0:T(8,128)(2,1)S(1)}, bf16[2,2,8,2,8,128]{5,4,3,2,1,0:T(8,128)(2,1)}, u32[]{:S(2)}) copy-start(bf16[2,2,8,2,8,128]{5,4,3,2,1,0:T(8,128)(2,1)} %copy-done.40) | copy-start | bytes 393220
  84.5 3.1 %copy-start.39 = (bf16[2,2,8,2,8,128]{5,4,3,2,1,0:T(8,128)(2,1)S(1)}, bf16[2,2,8,2,8,128]{5,4,3,2,1,0:T(8,128)(2,1)}, u32[]{:S(2)}) copy-start(bf16[2,2,8,2,8,128]{5,4,3,2,1,0:T(8,128)(2,1)} %copy-done.38) | copy-start | bytes 393220
  87.2 3.9 %copy-start.55 = (bf16[2,2,64,2,128]{4,2,3,1,0:T(8,128)(2,1)S(1)}, bf16[2,2,64,2,128]{4,2,3,1,0:T(8,128)(2,1)}, u32[]{:S(2)}) copy-start(bf16[2,2,64,2,128]{4,2,3,1,0:T(8,128)(2,1)} %get-tuple-element.145) | copy-start | bytes 393220
  87.7 3.8 %copy-start.49 = (bf16[16,16,256]{2,1,0:T(8,128)(2,1)S(1)}, bf16[16,16,256]{2,1,0:T(8,128)(2,1)}, u32[]{:S(2)}) copy-start(bf16[16,16,256]{2,1,0:T(8,128)(2,1)} %param.17) | copy-start | bytes 393220
  88.7 5.5 %collective-permute-start.8 = (f32[8,16,4]{1,0,2:T(8,128)S(1)}, f32[8,16,4]{1,0,2:T(8,128)S(1)}, u32[]{:S(2)}, u32[]{:S(2)}) collective-permute-start(f32[8,16,4]{1,0,2:T(8,128)S(1)} %slice.401), channel_id=1, source_target_pairs={{0,4},{4,8},{8,12},{12,16},{16,20},{20,24},{24,28},{1,5},{5,9},{9,... | collective-permute-start | bytes 6152 | tf_op jit(solution)/shard_map/ppermute | solution.py:20
  91.4 14.9 %copy-start.33 = (bf16[2,2,8,2,8,128]{5,4,3,2,1,0:T(8,128)(2,1)S(1)}, bf16[2,2,8,2,8,128]{5,4,3,2,1,0:T(8,128)(2,1)}, u32[]{:S(2)}) copy-start(bf16[2,2,8,2,8,128]{5,4,3,2,1,0:T(8,128)(2,1)} %copy-done.32) | copy-start | bytes 393220
  91.5 14.9 %copy-start.37 = (bf16[2,2,8,2,8,128]{5,4,3,2,1,0:T(8,128)(2,1)S(1)}, bf16[2,2,8,2,8,128]{5,4,3,2,1,0:T(8,128)(2,1)}, u32[]{:S(2)}) copy-start(bf16[2,2,8,2,8,128]{5,4,3,2,1,0:T(8,128)(2,1)} %get-tuple-element.64) | copy-start | bytes 393220
  91.5 14.9 %copy-start.78 = (pred[2,2]{1,0:T(4,128)(4,1)S(1)}, pred[2,2]{1,0:T(4,128)(4,1)}, u32[]{:S(2)}) copy-start(pred[2,2]{1,0:T(4,128)(4,1)} %copy-done.77) | copy-start | bytes 16
  92.5 14.1 %copy-start.8 = (bf16[2,2,8,2,8,128]{5,4,3,2,1,0:T(8,128)(2,1)S(1)}, bf16[2,2,8,2,8,128]{5,4,3,2,1,0:T(8,128)(2,1)}, u32[]{:S(2)}) copy-start(bf16[2,2,8,2,8,128]{5,4,3,2,1,0:T(8,128)(2,1)} %get-tuple-element.63) | copy-start | bytes 393220
  92.7 13.8 %copy-start.50 = (bf16[2,8,2,8,256]{4,3,2,1,0:T(8,128)(2,1)}, bf16[2,8,2,8,256]{4,3,2,1,0:T(8,128)(2,1)S(1)}, u32[]{:S(2)}) copy-start(bf16[2,8,2,8,256]{4,3,2,1,0:T(8,128)(2,1)S(1)} %copy.449) | copy-start | bytes 393220
  93.0 6.0 %collective-permute-start.9 = (f32[8,16,4]{1,0,2:T(8,128)S(1)}, f32[8,16,4]{1,0,2:T(8,128)S(1)}, u32[]{:S(2)}, u32[]{:S(2)}) collective-permute-start(f32[8,16,4]{1,0,2:T(8,128)S(1)} %slice.403), channel_id=1, source_target_pairs={{4,0},{8,4},{12,8},{16,12},{20,16},{24,20},{28,24},{5,1},{9,5},{13... | collective-permute-start | bytes 6152 | tf_op jit(solution)/shard_map/ppermute | solution.py:23
  99.1 3.7 %collective-permute-start.10 = (f32[32,8,4]{1,0,2:T(8,128)S(1)}, f32[32,8,4]{1,0,2:T(8,128)S(1)}, u32[]{:S(2)}, u32[]{:S(2)}) collective-permute-start(f32[32,8,4]{1,0,2:T(8,128)S(1)} %get-tuple-element.93), channel_id=1, source_target_pairs={{0,1},{1,2},{2,3},{4,5},{5,6},{6,7},{8,9},{9,10},{10,11},{12,13},{... | collective-permute-start | bytes 12296 | tf_op jit(solution)/shard_map/ppermute | solution.py:20
  100.4 4.9 %collective-permute-start.11 = (f32[32,8,4]{1,0,2:T(8,128)S(1)}, f32[32,8,4]{1,0,2:T(8,128)S(1)}, u32[]{:S(2)}, u32[]{:S(2)}) collective-permute-start(f32[32,8,4]{1,0,2:T(8,128)S(1)} %get-tuple-element.94), channel_id=1, source_target_pairs={{1,0},{2,1},{3,2},{5,4},{6,5},{7,6},{9,8},{10,9},{11,10},{13,12},{... | collective-permute-start | bytes 12296 | tf_op jit(solution)/shard_map/ppermute | solution.py:23
  101.8 5.3 %copy-start.53 = (bf16[2,2,8,2,8,128]{5,4,3,2,1,0:T(8,128)(2,1)S(1)}, bf16[2,2,8,2,8,128]{5,4,3,2,1,0:T(8,128)(2,1)}, u32[]{:S(2)}) copy-start(bf16[2,2,8,2,8,128]{5,4,3,2,1,0:T(8,128)(2,1)} %get-tuple-element.48) | copy-start | bytes 393220
  101.8 5.3 %copy-start.76 = (pred[2,2]{1,0:T(4,128)(4,1)S(1)}, pred[2,2]{1,0:T(4,128)(4,1)}, u32[]{:S(2)}) copy-start(pred[2,2]{1,0:T(4,128)(4,1)} %copy-done.75) | copy-start | bytes 16
  110.5 6.6 %copy-start.23 = (f32[2,2,2,64,64]{3,4,2,1,0:T(8,128)S(1)}, f32[2,2,2,64,64]{3,4,2,1,0:T(8,128)}, u32[]{:S(2)}) copy-start(f32[2,2,2,64,64]{3,4,2,1,0:T(8,128)} %copy-done.22) | copy-start | bytes 393220
  118.5 3.8 %copy-start.29 = (bf16[2,2,8,2,8,128]{5,4,3,2,1,0:T(8,128)(2,1)S(1)}, bf16[2,2,8,2,8,128]{5,4,3,2,1,0:T(8,128)(2,1)}, u32[]{:S(2)}) copy-start(bf16[2,2,8,2,8,128]{5,4,3,2,1,0:T(8,128)(2,1)} %get-tuple-element.52) | copy-start | bytes 393220
  118.5 4.1 %copy-start.27 = (bf16[2,2,8,2,8,128]{5,4,3,2,1,0:T(8,128)(2,1)S(1)}, bf16[2,2,8,2,8,128]{5,4,3,2,1,0:T(8,128)(2,1)}, u32[]{:S(2)}) copy-start(bf16[2,2,8,2,8,128]{5,4,3,2,1,0:T(8,128)(2,1)} %get-tuple-element.50) | copy-start | bytes 393220
  119.7 3.2 %copy-start.54 = (bf16[2,2,8,2,8,128]{5,4,3,2,1,0:T(8,128)(2,1)S(1)}, bf16[2,2,8,2,8,128]{5,4,3,2,1,0:T(8,128)(2,1)}, u32[]{:S(2)}) copy-start(bf16[2,2,8,2,8,128]{5,4,3,2,1,0:T(8,128)(2,1)} %get-tuple-element.48) | copy-start | bytes 393220
  122.3 2.3 copy-start.52
  123.3 40.5 %copy-start.25 = (bf16[256,256]{1,0:T(8,128)(2,1)S(1)}, bf16[256,256]{1,0:T(8,128)(2,1)}, u32[]{:S(2)}) copy-start(bf16[256,256]{1,0:T(8,128)(2,1)} %param.13) | copy-start | bytes 393220
  123.4 41.2 %copy-start.51 = (bf16[2,8,2,8,256]{4,3,2,1,0:T(8,128)(2,1)S(1)}, bf16[2,8,2,8,256]{4,3,2,1,0:T(8,128)(2,1)}, u32[]{:S(2)}) copy-start(bf16[2,8,2,8,256]{4,3,2,1,0:T(8,128)(2,1)} %copy-done.50) | copy-start | bytes 393220
  123.4 41.2 %copy-start.56 = (bf16[256,256]{1,0:T(8,128)(2,1)S(1)}, bf16[256,256]{1,0:T(8,128)(2,1)}, u32[]{:S(2)}) copy-start(bf16[256,256]{1,0:T(8,128)(2,1)} %param.12) | copy-start | bytes 393220
  123.4 41.2 %copy-start.57 = (bf16[256,256]{1,0:T(8,128)(2,1)S(1)}, bf16[256,256]{1,0:T(8,128)(2,1)}, u32[]{:S(2)}) copy-start(bf16[256,256]{1,0:T(8,128)(2,1)} %param.11) | copy-start | bytes 393220
  123.5 41.2 %copy-start.58 = (bf16[256,256]{1,0:T(8,128)(2,1)S(1)}, bf16[256,256]{1,0:T(8,128)(2,1)}, u32[]{:S(2)}) copy-start(bf16[256,256]{1,0:T(8,128)(2,1)} %param.10) | copy-start | bytes 393220
  125.5 122.0 %all-reduce.5.cloned.1.call-start = ((), (), s32[]{:S(2)}) async-start(), calls=%async_computation.1 | async-start | bytes 2097152 | tf_op jit(solution)/shard_map/psum | solution.py:245
  (30 other events, 46.5 us)
Sparse Core Ops, SparseCore 0:
  10.2 55.1 all-gather.2
  125.6 38.1 all-reduce.6
  168.1 79.3 all-reduce.4
